TPU v7x, 256 devices: a whole 4x4x8 slice. The times are simulated.
256 devices in a mesh: seq: 128 (over x, y, z), head: 2 (over core).
Axes of the slice: x: 4, y: 4, z: 8, core: 2. Of those that a mesh axis runs over, the one named last changes fastest.
Arguments:
- queries: bfloat16 [32768, 4096], P('seq', 'head'), may hold values from -12 to 12
- key_states: bfloat16 [32768, 1024], P('seq', 'head'), may hold values from -12 to 12
- value_states: bfloat16 [32768, 1024], P('seq', 'head'), may hold values from -6 to 6
- positions: int32 [3, 32768], P(None, 'seq'), may hold values from 0 to 4095
- random_blocks: int32 [512, 8, 3], P('seq', 'head'), may hold values from 0 to 511, as said below
- global_blocks: int32 [2], replicated, may hold values from 0 to 511
- out_grad: bfloat16 [32768, 4096], P('seq', 'head'), may hold values from -6 to 6
Outputs:
- attended: bfloat16 [32768, 4096], P('seq', 'head')
- query_grad: bfloat16 [32768, 4096], P('seq', 'head')
- key_grad: bfloat16 [32768, 1024], P('seq', 'head')
- value_grad: bfloat16 [32768, 1024], P('seq', 'head')
Inputs may be any that keep to these rules, and one draw needn't show every extreme that they name: `random_blocks`: for each index of seq and each index of head (its 4 block rows and 4 key-value heads), at most 2 of its random blocks lie in the blocks of any one index of seq, and exactly 2 in one of them.
All inputs are finite; a program needn't handle non-finite values.
Results may differ from a plain program's by a relative error of at most 0.013.
The roundings to bfloat16 on the way count: a program that leaves them out, or rounds other values in their place, can miss the bound.
Values may be sent and summed in bfloat16 or wider, within the bound.
No kernel may reach another device: no remote copies, remote signals or barrier semaphores. Data moves between devices by JAX's collectives and lax.ppermute only.
A program may use at most 128 MiB of HBM per device.

v0:
```python
import math
import jax
import jax.numpy as jnp
from jax import lax
from jax.sharding import PartitionSpec as P

HD = 128
GROUP = 4
BLK = 64
GLOB = 2
RND = 3
NEG_FILL = -1e30
ROPE_BASE = 1000000.0


def extended(array, sides, width):
    for axis, dim in sides:
        devices, length = (lax.axis_size(axis), array.shape[dim])
        up = [(i, (i + 1) % devices) for i in range(devices - 1)]
        down = [(j, i) for i, j in up]
        last = lax.slice_in_dim(array, length - width, length, axis=dim)
        leading = lax.slice_in_dim(array, 0, width, axis=dim)
        before = lax.ppermute(last, axis, up)
        after = lax.ppermute(leading, axis, down)
        array = jnp.concatenate([before, array, after], axis=dim)
    return array


def spread(block, axis, source):
    block = jnp.where(lax.axis_index(axis) == source, block, jnp.zeros_like(block))
    return lax.psum(block, axis)


def shifted(array, axis, by):
    devices = lax.axis_size(axis)
    pairs = [(i, i + by) for i in range(devices) if 0 <= i + by < devices]
    return lax.ppermute(array, axis, pairs)


def tables(positions):
    half_dim = HD // 2
    freq_ids = jnp.arange(half_dim)
    inv_freq = jnp.power(jnp.float32(ROPE_BASE), -2.0 * freq_ids.astype(jnp.float32) / HD)
    pos_float = positions.astype(jnp.float32)
    chosen = jnp.where(
        (freq_ids % 3 == 0)[None, :],
        pos_float[0][:, None],
        jnp.where((freq_ids % 3 == 1)[None, :], pos_float[1][:, None], pos_float[2][:, None]),
    )
    angles = chosen * inv_freq[None, :]
    return (jnp.cos(angles), jnp.sin(angles))


def rotate(states, cosines, sine_vals):
    half_dim = HD // 2
    first_half = states[..., :half_dim]
    second_half = states[..., half_dim:]
    cos_b = cosines[:, None, :]
    sin_b = sine_vals[:, None, :]
    return jnp.concatenate(
        [first_half * cos_b - second_half * sin_b, second_half * cos_b + first_half * sin_b],
        axis=-1,
    )


def unrotate(states, cosines, sine_vals):
    half_dim = HD // 2
    first_half = states[..., :half_dim]
    second_half = states[..., half_dim:]
    cos_b = cosines[:, None, :]
    sin_b = sine_vals[:, None, :]
    return jnp.concatenate(
        [first_half * cos_b + second_half * sin_b, second_half * cos_b - first_half * sin_b],
        axis=-1,
    )


def attend(query_block_view, key_block_view, value_block_view, gradient_block_view, key_mask):
    score_scale = 1.0 / math.sqrt(HD)
    logit_scores = (
        jnp.einsum(
            "mtyp,mop->myto", query_block_view, key_block_view, preferred_element_type=jnp.float32
        )
        * score_scale
    )
    logit_scores = jnp.where(key_mask[:, None, None, :], logit_scores, NEG_FILL)
    row_max = jnp.max(logit_scores, axis=-1, keepdims=True)
    exponent = jnp.exp(logit_scores - row_max)
    probability = exponent / jnp.sum(exponent, axis=-1, keepdims=True)
    attention_weights = probability.astype(jnp.bfloat16)
    attended = jnp.einsum(
        "ywiu,yuz->yiwz", attention_weights, value_block_view, preferred_element_type=jnp.float32
    ).astype(jnp.bfloat16)
    weight_gradient = jnp.einsum(
        "mtyp,mop->myto", gradient_block_view, value_block_view, preferred_element_type=jnp.float32
    )
    row_delta = jnp.sum(
        gradient_block_view.astype(jnp.float32) * attended.astype(jnp.float32), axis=-1
    )
    row_delta = jnp.transpose(row_delta, (0, 2, 1))[..., None]
    score_gradient = (probability * (weight_gradient - row_delta) * score_scale).astype(
        jnp.bfloat16
    )
    value_portion = jnp.einsum(
        "pcht,phca->pta", attention_weights, gradient_block_view, preferred_element_type=jnp.float32
    )
    key_portion = jnp.einsum(
        "pcht,phca->pta", score_gradient, query_block_view, preferred_element_type=jnp.float32
    )
    query_portion = jnp.einsum(
        "ywiu,yuz->yiwz", score_gradient, key_block_view, preferred_element_type=jnp.float32
    )
    return (attended, query_portion, key_portion, value_portion)


def onehot(ids, count):
    return (ids[:, None] == jnp.arange(count, dtype=jnp.int32)[None, :]).astype(jnp.bfloat16)


def local(queries, key_states, value_states, positions, random_blocks, global_blocks, out_grad):
    tok_rows = queries.shape[0]
    block_rows = tok_rows // BLK
    kv_dev = key_states.shape[1] // HD
    seq_count = lax.axis_size("seq")
    my_index = lax.axis_index("seq")
    slot_count = block_rows * kv_dev * RND
    capacity = (slot_count + seq_count - 1) // seq_count + 1
    score_scale = 1.0 / math.sqrt(HD)
    table_rows = block_rows * kv_dev
    all_blocks = lax.all_gather(random_blocks, "seq").reshape(seq_count, slot_count)
    head_ids = jnp.broadcast_to(
        jnp.arange(kv_dev, dtype=jnp.int32)[None, :, None], (block_rows, kv_dev, RND)
    ).reshape(slot_count)
    slot_ids = jnp.arange(slot_count, dtype=jnp.int32)
    all_owners = all_blocks // block_rows
    earlier = (all_owners[:, :, None] == all_owners[:, None, :]) & (
        slot_ids[None, None, :] < slot_ids[None, :, None]
    )
    all_rank = jnp.sum(earlier, axis=2)
    all_code = all_blocks % block_rows * kv_dev + head_ids[None, :]
    mine = all_owners == my_index
    asked_part = jnp.stack(
        [jnp.sum(jnp.where(mine & (all_rank == c), all_code, 0), axis=1) for c in range(capacity)],
        axis=1,
    )
    flat_ids = random_blocks.reshape(slot_count)
    owners = flat_ids // block_rows
    my_rank = lax.dynamic_index_in_dim(all_rank, my_index, 0, keepdims=False)
    slot_pos = owners * capacity + my_rank
    cosines, sine_vals = tables(positions)
    q_rot = rotate(
        queries.reshape(tok_rows, kv_dev * GROUP, HD).astype(jnp.float32), cosines, sine_vals
    ).astype(jnp.bfloat16)
    k_rot = rotate(
        key_states.reshape(tok_rows, kv_dev, HD).astype(jnp.float32), cosines, sine_vals
    ).astype(jnp.bfloat16)
    paired = jnp.stack([k_rot.reshape(tok_rows, kv_dev * HD), value_states])
    own_blocks = paired.reshape(2, block_rows, BLK, kv_dev, HD)
    kv_table = own_blocks.transpose(1, 3, 0, 2, 4).reshape(table_rows, 2 * BLK * HD)
    asked_flat = asked_part.reshape(seq_count * capacity)
    answers = jnp.dot(
        onehot(asked_flat, table_rows), kv_table, preferred_element_type=jnp.float32
    ).astype(jnp.bfloat16)
    padded = extended(paired, (("seq", 1),), BLK)
    window_blocks = padded.reshape(2, block_rows + 2, BLK, kv_dev, HD)
    glob_owner = global_blocks // block_rows
    glob_local = global_blocks % block_rows
    glob_pieces = []
    for which_glob in range(GLOB):
        glob_piece = lax.dynamic_index_in_dim(own_blocks, glob_local[which_glob], 1, keepdims=False)
        glob_pieces.append(spread(glob_piece, "seq", glob_owner[which_glob]))
    glob_kv = jnp.stack(glob_pieces, axis=1)
    answers, padded, glob_kv = lax.optimization_barrier((answers, padded, glob_kv))
    window_blocks = padded.reshape(2, block_rows + 2, BLK, kv_dev, HD)
    fetched = lax.all_to_all(
        answers.reshape(seq_count, capacity, 2 * BLK * HD), "seq", 0, 0, tiled=True
    ).reshape(seq_count * capacity, 2 * BLK * HD)
    window_set = jnp.stack(
        [window_blocks[:, offset : offset + block_rows] for offset in range(3)], axis=2
    )
    glob_set = jnp.broadcast_to(glob_kv[:, None], (2, block_rows, GLOB, BLK, kv_dev, HD))
    near_set = jnp.concatenate([window_set, glob_set], axis=2).reshape(
        2, block_rows, (3 + GLOB) * BLK, kv_dev, HD
    )
    window_ids = (
        my_index * block_rows + jnp.arange(block_rows)[:, None] + jnp.arange(-1, 2)[None, :]
    )
    window_ok = (window_ids >= 0) & (window_ids < seq_count * block_rows)
    near_ok = jnp.concatenate([window_ok, jnp.ones((block_rows, GLOB), dtype=bool)], axis=1)
    near_mask = jnp.repeat(near_ok, BLK, axis=1)
    query_nat = q_rot.reshape(block_rows, BLK, kv_dev, GROUP, HD)
    grad_nat = out_grad.reshape(block_rows, BLK, kv_dev, GROUP, HD)
    near_k = near_set[0]
    near_v = near_set[1]
    near_scores = (
        jnp.einsum("rthgd,rkhd->rhgtk", query_nat, near_k, preferred_element_type=jnp.float32)
        * score_scale
    )
    near_scores = jnp.where(near_mask[:, None, None, None, :], near_scores, NEG_FILL)
    near_wgrad = jnp.einsum(
        "rthgd,rkhd->rhgtk", grad_nat, near_v, preferred_element_type=jnp.float32
    )
    random_kv = fetched[slot_pos].reshape(block_rows, kv_dev, RND, 2, BLK, HD)
    far_k = random_kv[:, :, :, 0].reshape(block_rows, kv_dev, RND * BLK, HD)
    far_v = random_kv[:, :, :, 1].reshape(block_rows, kv_dev, RND * BLK, HD)
    far_scores = (
        jnp.einsum("rthgd,rhkd->rhgtk", query_nat, far_k, preferred_element_type=jnp.float32)
        * score_scale
    )
    far_wgrad = jnp.einsum("rthgd,rhkd->rhgtk", grad_nat, far_v, preferred_element_type=jnp.float32)
    row_max = jnp.maximum(
        jnp.max(near_scores, axis=-1, keepdims=True), jnp.max(far_scores, axis=-1, keepdims=True)
    )
    near_exp = jnp.exp(near_scores - row_max)
    far_exp = jnp.exp(far_scores - row_max)
    total = jnp.sum(near_exp, axis=-1, keepdims=True) + jnp.sum(far_exp, axis=-1, keepdims=True)
    near_prob = near_exp / total
    far_prob = far_exp / total
    near_w = near_prob.astype(jnp.bfloat16)
    far_w = far_prob.astype(jnp.bfloat16)
    attended = (
        jnp.einsum("rhgtk,rkhd->rthgd", near_w, near_v, preferred_element_type=jnp.float32)
        + jnp.einsum("rhgtk,rhkd->rthgd", far_w, far_v, preferred_element_type=jnp.float32)
    ).astype(jnp.bfloat16)
    row_delta = jnp.sum(grad_nat.astype(jnp.float32) * attended.astype(jnp.float32), axis=-1)
    row_delta = row_delta.transpose(0, 2, 3, 1)[..., None]
    near_sgrad = (near_prob * (near_wgrad - row_delta) * score_scale).astype(jnp.bfloat16)
    far_sgrad = (far_prob * (far_wgrad - row_delta) * score_scale).astype(jnp.bfloat16)
    far_kgrad = jnp.einsum(
        "rhgtk,rthgd->rhkd", far_sgrad, query_nat, preferred_element_type=jnp.float32
    )
    far_vgrad = jnp.einsum("rhgtk,rthgd->rhkd", far_w, grad_nat, preferred_element_type=jnp.float32)
    random_grad = (
        jnp.stack(
            [
                far_kgrad.reshape(block_rows, kv_dev, RND, BLK, HD),
                far_vgrad.reshape(block_rows, kv_dev, RND, BLK, HD),
            ],
            axis=3,
        )
        .reshape(slot_count, 2 * BLK * HD)
        .astype(jnp.bfloat16)
    )
    outgoing = jnp.dot(
        onehot(slot_pos, seq_count * capacity).T, random_grad, preferred_element_type=jnp.float32
    ).astype(jnp.bfloat16)
    query_portion = jnp.einsum(
        "rhgtk,rkhd->rthgd", near_sgrad, near_k, preferred_element_type=jnp.float32
    ) + jnp.einsum("rhgtk,rhkd->rthgd", far_sgrad, far_k, preferred_element_type=jnp.float32)
    near_kgrad = jnp.einsum(
        "rhgtk,rthgd->rkhd", near_sgrad, query_nat, preferred_element_type=jnp.float32
    )
    near_vgrad = jnp.einsum(
        "rhgtk,rthgd->rkhd", near_w, grad_nat, preferred_element_type=jnp.float32
    )
    near_grad = jnp.stack([near_kgrad, near_vgrad]).reshape(
        2, block_rows, 3 + GLOB, BLK, kv_dev, HD
    )
    window_acc = jnp.pad(near_grad[:, :, 0], ((0, 0), (0, 2), (0, 0), (0, 0), (0, 0)))
    window_acc = window_acc + jnp.pad(near_grad[:, :, 1], ((0, 0), (1, 1), (0, 0), (0, 0), (0, 0)))
    window_acc = window_acc + jnp.pad(near_grad[:, :, 2], ((0, 0), (2, 0), (0, 0), (0, 0), (0, 0)))
    glob_local_grad = jnp.sum(near_grad[:, :, 3:], axis=1)
    from_right = shifted(window_acc[:, 0].astype(jnp.bfloat16), "seq", -1).astype(jnp.float32)
    from_left = shifted(window_acc[:, block_rows + 1].astype(jnp.bfloat16), "seq", 1).astype(
        jnp.float32
    )
    glob_grad = lax.psum(glob_local_grad, "seq")
    outgoing, from_right, from_left, glob_grad = lax.optimization_barrier(
        (outgoing, from_right, from_left, glob_grad)
    )
    returned = lax.all_to_all(
        outgoing.reshape(seq_count, capacity, 2 * BLK * HD), "seq", 0, 0, tiled=True
    ).reshape(seq_count * capacity, 2 * BLK * HD)
    kv_grad = window_acc[:, 1 : block_rows + 1]
    kv_grad = kv_grad.at[:, block_rows - 1].add(from_right).at[:, 0].add(from_left)
    glob_mine = jnp.where((glob_owner == my_index)[None, :, None, None, None], glob_grad, 0.0)
    kv_grad = kv_grad.at[:, glob_local].add(glob_mine)
    collected = jnp.dot(
        onehot(asked_flat, table_rows).T, returned, preferred_element_type=jnp.float32
    ).reshape(block_rows, kv_dev, 2, BLK, HD)
    kv_grad = kv_grad + collected.transpose(2, 0, 3, 1, 4)
    attended = attended.reshape(tok_rows, kv_dev * GROUP * HD)
    query_grad = (
        unrotate(query_portion.reshape(tok_rows, kv_dev * GROUP, HD), cosines, sine_vals)
        .astype(jnp.bfloat16)
        .reshape(tok_rows, kv_dev * GROUP * HD)
    )
    key_acc = kv_grad[0].reshape(tok_rows, kv_dev, HD)
    key_grad = (
        unrotate(key_acc, cosines, sine_vals).astype(jnp.bfloat16).reshape(tok_rows, kv_dev * HD)
    )
    value_grad = kv_grad[1].reshape(tok_rows, kv_dev * HD).astype(jnp.bfloat16)
    return (attended, query_grad, key_grad, value_grad)


def solution(mesh):
    in_specs = (
        P("seq", "head"),
        P("seq", "head"),
        P("seq", "head"),
        P(None, "seq"),
        P("seq", "head", None),
        P(),
        P("seq", "head"),
    )
    out_specs = (P("seq", "head"), P("seq", "head"), P("seq", "head"), P("seq", "head"))
    return jax.shard_map(local, mesh=mesh, in_specs=in_specs, out_specs=out_specs, check_vma=False)
```

profile of v0, /device:TPU:32, one launch (start us, length us, event | category | flops | bytes accessed | tf_op | source)
XLA Modules:
  0.0 1072.5 jit_solution(8341888297970544012)
XLA Ops:
  8.0 1.1 copy.289
  9.1 1.1 copy.293
  10.6 0.9 fusion.30
  11.5 3.8 collective-permute-start
  15.4 2.7 collective-permute-start.1
  27.1 348.5 %all-gather = s32[512,4,3]{2,1,0:T(4,128)S(1)} all-gather(s32[4,4,3]{2,1,0:T(4,128)S(1)} %copy.280), channel_id=2, replica_groups=mesh['seq'=128,'head'=2] {'seq'}, dimensions={0}, use_global_device_ids=true | all-gather | bytes 24768 | tf_op jit(solution)/shard_map/all_gather | solution.py:130
  375.6 1.0 reshape.601
  378.6 3.4 copy.336
  382.1 1.2 select_reduce_fusion.1
  383.5 5.7 convolution_convert_fusion.1
  389.2 2.4 pad_maximum_fusion.4
  391.5 1.0 pad_maximum_fusion.7
  392.5 14.2 %reshape.604 = bf16[128,2,16384]{2,1,0:T(2,128)(2,1)} reshape(bf16[256,16384]{1,0:T(8,128)(2,1)} %convolution_convert_fusion.1) | data formatting | bytes 16777216 | tf_op jit(solution)/shard_map/reshape | solution.py:176
  406.7 14.0 %all-to-all-start = ((bf16[128,2,16384]{2,1,0:T(2,128)(2,1)}), bf16[128,2,16384]{2,1,0:T(2,128)(2,1)}, u32[]{:S(2)}, u32[]{:S(2)}) async-start(bf16[128,2,16384]{2,1,0:T(2,128)(2,1)} %reshape.604), calls=%async_computation | async-start | bytes 16777216 | tf_op jit(solution)/shard_map/all_to_all | solution.py:175
  421.9 1.5 reshape.609
  425.0 0.8 copy.299
  426.2 0.8 copy.300
  427.0 0.9 dynamic-slice_reduce_fusion
  429.2 1.4 copy.294
  432.5 1.7 fusion.54
  434.2 1.1 copy-done.3
  435.3 3.7 bitcast_reduce_fusion
  439.0 112.6 %all-to-all-done = bf16[128,2,16384]{2,1,0:T(2,128)(2,1)} async-done(((bf16[128,2,16384]{2,1,0:T(2,128)(2,1)}), bf16[128,2,16384]{2,1,0:T(2,128)(2,1)}, u32[]{:S(2)}, u32[]{:S(2)}) %all-to-all-start) | async-done | bytes 8388640 | tf_op jit(solution)/shard_map/all_to_all | solution.py:175
  551.5 13.1 %reshape.605 = bf16[256,16384]{1,0:T(8,128)(2,1)} reshape(bf16[128,2,16384]{2,1,0:T(2,128)(2,1)} %all-to-all-done) | data formatting | bytes 16777216 | tf_op jit(solution)/shard_map/reshape | solution.py:177
  564.7 7.4 gather_fusion
  572.6 0.8 bitcast_reduce_fusion.1
  573.5 1.5 fusion.11
  575.6 1.9 fusion.5
  577.6 3.6 bitcast_convert_fusion
  581.2 2.1 fusion.14
  583.3 3.0 multiply_reduce_fusion
  586.3 2.1 fusion.8
  588.4 2.8 fusion.2
  591.3 4.0 fusion.12
  595.3 1.1 fusion.62
  596.3 2.0 copy_dynamic-update-slice_fusion.1
  598.3 2.1 copy_dynamic-update-slice_fusion
  600.4 2.3 copy-done.2
  602.7 1.1 slice_reduce_fusion
  603.9 2.1 slice_bitcast_fusion.2
  606.0 1.8 bitcast_convert_fusion.1
  607.8 1.8 fusion.53
  610.3 1.3 pad_maximum_fusion.1
  612.3 1.9 collective-permute-start.3
  614.3 3.9 collective-permute-start.2
  618.2 5.7 convolution_convert_fusion
  624.7 197.6 %all-reduce.8.cloned.1.call-done = f32[2,2,64,4,128]{4,3,2,0,1:T(4,128)} async-done(((f32[2,2,64,4,128]{4,3,2,0,1:T(4,128)}), f32[2,2,64,4,128]{4,3,2,0,1:T(4,128)}) %all-reduce.8.cloned.1.call-update) | async-done | bytes 524304 | tf_op jit(solution)/shard_map/psum | solution.py:267
  822.3 14.2 %reshape.614 = bf16[128,2,16384]{2,1,0:T(2,128)(2,1)} reshape(bf16[256,16384]{1,0:T(8,128)(2,1)} %convolution_convert_fusion) | data formatting | bytes 16777216 | tf_op jit(solution)/shard_map/reshape | solution.py:272
  836.5 11.2 %all-to-all-start.1 = ((bf16[128,2,16384]{2,1,0:T(2,128)(2,1)}), bf16[128,2,16384]{2,1,0:T(2,128)(2,1)}, u32[]{:S(2)}, u32[]{:S(2)}) async-start(bf16[128,2,16384]{2,1,0:T(2,128)(2,1)} %reshape.614), calls=%async_computation.1 | async-start | bytes 16777216 | tf_op jit(solution)/shard_map/all_to_all | solution.py:271
  847.7 3.2 copy.304
  851.0 2.6 reshape.608
  853.6 2.4 fusion.61
  857.0 2.1 fusion.55
  859.1 2.2 copy.340
  861.2 1.6 copy.339
  862.8 1.6 add_convert_fusion.1
  864.5 1.4 copy.325
  866.0 1.2 select_bitcast_fusion
  867.5 163.5 %all-to-all-done.1 = bf16[128,2,16384]{2,1,0:T(2,128)(2,1)} async-done(((bf16[128,2,16384]{2,1,0:T(2,128)(2,1)}), bf16[128,2,16384]{2,1,0:T(2,128)(2,1)}, u32[]{:S(2)}, u32[]{:S(2)}) %all-to-all-start.1) | async-done | bytes 8388640 | tf_op jit(solution)/shard_map/all_to_all | solution.py:271
  1031.0 13.1 %reshape.615 = bf16[256,16384]{1,0:T(8,128)(2,1)} reshape(bf16[128,2,16384]{2,1,0:T(2,128)(2,1)} %all-to-all-done.1) | data formatting | bytes 16777216 | tf_op jit(solution)/shard_map/reshape | solution.py:273
  1044.2 12.0 %copy.318 = bf16[256,16384]{0,1:T(8,128)(2,1)} copy(bf16[256,16384]{1,0:T(8,128)(2,1)} %reshape.615) | data formatting | bytes 16777216 | tf_op jit(solution)/shard_map/reshape | solution.py:273
  1056.2 5.7 fusion.17
  1062.0 0.8 scatter_fusion
  1064.6 0.8 copy.326
  (137 shorter events, 20.0 us)
Async XLA Ops:
  7.2 14.8 %copy-start.15 = (bf16[256,512]{1,0:T(8,128)(2,1)S(1)}, bf16[256,512]{1,0:T(8,128)(2,1)}, u32[]{:S(2)}) copy-start(bf16[256,512]{1,0:T(8,128)(2,1)} %param.13) | copy-start | bytes 786436
  7.2 10.9 %copy-start.20 = (s32[2]{0:T(128)S(1)}, s32[2]{0:T(128)}, u32[]{:S(2)}) copy-start(s32[2]{0:T(128)} %param.16) | copy-start | bytes 28
  7.2 384.4 %all-reduce.10.cloned.1.call-start = ((), (), s32[]{:S(2)}) async-start(), calls=%async_computation.3 | async-start | bytes 524288 | tf_op jit(solution)/shard_map/psum | solution.py:31
  10.5 16.2 %copy-start.17 = (s32[4,4,3]{1,0,2:T(4,128)S(1)}, s32[4,4,3]{1,0,2:T(4,128)}, u32[]{:S(2)}) copy-start(s32[4,4,3]{1,0,2:T(4,128)} %param.15) | copy-start | bytes 580
  11.5 377.6 %collective-permute-start = (bf16[2,64,512]{1,2,0:T(8,128)(2,1)}, bf16[2,64,512]{1,2,0:T(8,128)(2,1)}, u32[]{:S(2)}, u32[]{:S(2)}) collective-permute-start(bf16[2,64,512]{1,2,0:T(8,128)(2,1)} %get-tuple-element.102), channel_id=1, source_target_pairs={{0,2},{2,4},{4,6},{6,8},{8,10},{10,12},{12,14},{14,16},{16,18},{18... | collective-permute-start | bytes 393224 | tf_op jit(solution)/shard_map/ppermute | solution.py:23
  15.4 373.8 %collective-permute-start.1 = (bf16[2,64,512]{1,2,0:T(8,128)(2,1)}, bf16[2,64,512]{1,2,0:T(8,128)(2,1)}, u32[]{:S(2)}, u32[]{:S(2)}) collective-permute-start(bf16[2,64,512]{1,2,0:T(8,128)(2,1)} %get-tuple-element.103), channel_id=1, source_target_pairs={{2,0},{4,2},{6,4},{8,6},{10,8},{12,10},{14,12},{16,14},{18,16},{20... | collective-permute-start | bytes 393224 | tf_op jit(solution)/shard_map/ppermute | solution.py:24
  377.2 0.6 copy-start.16
  406.7 15.2 %copy-start.12 = (bf16[256,2048]{1,0:T(8,128)(2,1)S(1)}, bf16[256,2048]{1,0:T(8,128)(2,1)}, u32[]{:S(2)}) copy-start(bf16[256,2048]{1,0:T(8,128)(2,1)} %param.17) | copy-start | bytes 3145732
  406.7 16.7 %copy-start.13 = (bf16[256,2048]{1,0:T(8,128)(2,1)S(1)}, bf16[256,2048]{1,0:T(8,128)(2,1)}, u32[]{:S(2)}) copy-start(bf16[256,2048]{1,0:T(8,128)(2,1)} %param.11) | copy-start | bytes 3145732
  406.7 144.8 %all-to-all-start = ((bf16[128,2,16384]{2,1,0:T(2,128)(2,1)}), bf16[128,2,16384]{2,1,0:T(2,128)(2,1)}, u32[]{:S(2)}, u32[]{:S(2)}) async-start(bf16[128,2,16384]{2,1,0:T(2,128)(2,1)} %reshape.604), calls=%async_computation | async-start | bytes 16777216 | tf_op jit(solution)/shard_map/all_to_all | solution.py:175
  420.7 401.6 %all-reduce.8.cloned.1.call-start = ((), (), s32[]{:S(2)}) async-start(), calls=%async_computation.2 | async-start | bytes 1048576 | tf_op jit(solution)/shard_map/psum | solution.py:267
  434.2 1.1 copy-start.3
  572.4 2.5 slice-start
  572.6 2.4 copy-start.6
  572.6 3.0 slice-start.1
  575.6 2.0 copy-start.14
  577.6 3.6 copy-start.10
  588.4 17.6 %copy-start.4 = (bf16[4,4,4,64,192]{4,3,2,1,0:T(8,128)(2,1)}, bf16[4,4,4,64,192]{4,3,2,1,0:T(8,128)(2,1)S(1)}, u32[]{:S(2)}) copy-start(bf16[4,4,4,64,192]{4,3,2,1,0:T(8,128)(2,1)S(1)} %fusion.8) | copy-start | bytes 4718596
  591.3 4.0 copy-start
  600.4 2.3 copy-start.2
  607.8 2.5 copy-start.9
  612.3 11.6 %collective-permute-start.3 = (bf16[2,64,4,128]{3,2,1,0:T(4,128)(2,1)S(1)}, bf16[2,64,4,128]{3,2,1,0:T(4,128)(2,1)S(1)}, u32[]{:S(2)}, u32[]{:S(2)}) collective-permute-start(bf16[2,64,4,128]{3,2,1,0:T(4,128)(2,1)S(1)} %get-tuple-element.89), channel_id=1, source_target_pairs={{0,2},{2,4},{4,6},{6,8},{8,10},{10,12},{12,14},{14,16},{16,18},{18... | collective-permute-start | bytes 393224 | tf_op jit(solution)/shard_map/ppermute | solution.py:37
  614.3 9.7 collective-permute-start.2
  836.5 194.6 %all-to-all-start.1 = ((bf16[128,2,16384]{2,1,0:T(2,128)(2,1)}), bf16[128,2,16384]{2,1,0:T(2,128)(2,1)}, u32[]{:S(2)}, u32[]{:S(2)}) async-start(bf16[128,2,16384]{2,1,0:T(2,128)(2,1)} %reshape.614), calls=%async_computation.1 | async-start | bytes 16777216 | tf_op jit(solution)/shard_map/all_to_all | solution.py:271
  847.7 5.9 copy-start.1
  853.6 2.4 copy-start.5
  853.6 2.4 copy-start.7
  862.8 3.2 copy-start.8
  864.4 1.6 copy-start.18
  866.0 1.4 copy-start.11
  1056.2 5.8 copy-start.19
Sparse Core Ops, SparseCore 0:
  26.8 218.4 all-reduce.9
  610.4 211.8 all-reduce.7
where the time goes:
time: 1080 us; the launch traced here: 1070 us
  waiting for transfers between devices  474 us (44%)
  blocking collectives  348 us (32%)
  local copies, waits for them, and re-layouts  123 us (11%)
  matrix products  45.1 us (4%)
  starting transfers between devices  37.8 us (3%)
  other arithmetic  23.6 us (2%)
  between operations  20.4 us (2%)
    all_gather x1, blocking collectives, local(): lax.all_gather(random_blocks, 'seq').reshape(seq_count, slot_count)  348 us
    psum x1, waiting for transfers between devices, local(): glob_grad = lax.psum(glob_local_grad, 'seq')  198 us
    all_to_all x1, waiting for transfers between devices, local(): lax.all_to_all(outgoing.reshape(seq_count, capacity, 2 * BLK * HD), 'seq'...  164 us
    all_to_all x1, waiting for transfers between devices, local(): lax.all_to_all(answers.reshape(seq_count, capacity, 2 * BLK * HD), 'seq',...  113 us
    reshape x2, local copies, waits for them, and re-layouts, local(): returned = lax.all_to_all(outgoing.reshape(seq_count, capacity, 2 * BLK *...  25.1 us
  transfers between devices with their start and end apart: 8, of which 3 were waited for; matrix products, arithmetic and copies ran while one was open for 6% of the time, Pallas kernels for 0%

commit v1 on v0

--- a/solution.py
+++ b/solution.py
@@ -264,7 +264,7 @@
     from_left = shifted(window_acc[:, block_rows + 1].astype(jnp.bfloat16), "seq", 1).astype(
         jnp.float32
     )
-    glob_grad = lax.psum(glob_local_grad, "seq")
+    glob_grad = lax.all_gather(glob_local_grad, "seq").sum(axis=0)
     outgoing, from_right, from_left, glob_grad = lax.optimization_barrier(
         (outgoing, from_right, from_left, glob_grad)
     )

time: 1080 us -> 1220 us (1.13)
  waiting for transfers between devices: 474 us -> 584 us
  other arithmetic: 23.6 us -> 44.3 us
    all_gather x0 -> x1, waiting for transfers between devices: none -> 305 us  [local(): glob_grad = lax.all_gather(glob_local_grad, 'seq').sum(axis=0)]
    psum x1 -> x0, waiting for transfers between devices: 198 us -> none  [local(): glob_grad = lax.psum(glob_local_grad, 'seq')]
    reduce_sum x0 -> x1, other arithmetic: none -> 21.7 us  [local(): glob_grad = lax.all_gather(glob_local_grad, 'seq').sum(axis=0)]
where the time goes in v1:
time: 1220 us; the launch traced here: 1210 us
  waiting for transfers between devices  584 us (48%)
  blocking collectives  348 us (29%)
  local copies, waits for them, and re-layouts  128 us (10%)
  matrix products  45.4 us (4%)
  other arithmetic  44.3 us (4%)
  starting transfers between devices  38.3 us (3%)
  between operations  20.3 us (2%)
    all_gather x1, blocking collectives, local(): lax.all_gather(random_blocks, 'seq').reshape(seq_count, slot_count)  348 us
    all_gather x1, waiting for transfers between devices, local(): glob_grad = lax.all_gather(glob_local_grad, 'seq').sum(axis=0)  305 us
    all_to_all x1, waiting for transfers between devices, local(): lax.all_to_all(outgoing.reshape(seq_count, capacity, 2 * BLK * HD), 'seq'...  166 us
    all_to_all x1, waiting for transfers between devices, local(): lax.all_to_all(answers.reshape(seq_count, capacity, 2 * BLK * HD), 'seq',...  114 us
    reshape x2, local copies, waits for them, and re-layouts, local(): returned = lax.all_to_all(outgoing.reshape(seq_count, capacity, 2 * BLK *...  25 us
  transfers between devices with their start and end apart: 8, of which 3 were waited for; matrix products, arithmetic and copies ran while one was open for 6% of the time, Pallas kernels for 0%

profile of v1, /device:TPU:32, one launch (start us, length us, event | category | flops | bytes accessed | tf_op | source)
XLA Modules:
  0.0 1208.7 jit_solution(12723237033564684314)
XLA Ops:
  8.0 1.1 copy.336
  9.1 1.1 copy.340
  10.6 0.9 fusion.30
  11.5 3.8 collective-permute-start
  15.4 2.7 collective-permute-start.1
  27.1 348.3 %all-gather = s32[512,4,3]{2,1,0:T(4,128)S(1)} all-gather(s32[4,4,3]{2,1,0:T(4,128)S(1)} %copy.327), channel_id=2, replica_groups=mesh['seq'=128,'head'=2] {'seq'}, dimensions={0}, use_global_device_ids=true | all-gather | bytes 24768 | tf_op jit(solution)/shard_map/all_gather | solution.py:130
  375.4 1.0 reshape.601
  378.4 3.4 copy.384
  381.9 1.2 select_reduce_fusion.1
  383.3 5.6 convolution_convert_fusion.1
  389.0 2.4 pad_maximum_fusion.4
  391.3 1.0 pad_maximum_fusion.7
  392.3 14.2 %reshape.604 = bf16[128,2,16384]{2,1,0:T(2,128)(2,1)} reshape(bf16[256,16384]{1,0:T(8,128)(2,1)} %convolution_convert_fusion.1) | data formatting | bytes 16777216 | tf_op jit(solution)/shard_map/reshape | solution.py:176
  406.5 14.0 %all-to-all-start = ((bf16[128,2,16384]{2,1,0:T(2,128)(2,1)}), bf16[128,2,16384]{2,1,0:T(2,128)(2,1)}, u32[]{:S(2)}, u32[]{:S(2)}) async-start(bf16[128,2,16384]{2,1,0:T(2,128)(2,1)} %reshape.604), calls=%async_computation | async-start | bytes 16777216 | tf_op jit(solution)/shard_map/all_to_all | solution.py:175
  421.1 1.5 reshape.609
  426.1 0.9 dynamic-slice_reduce_fusion
  428.2 1.4 copy.341
  431.5 1.6 fusion.54
  433.1 1.1 copy-done.5
  434.1 3.7 bitcast_reduce_fusion
  437.8 113.6 %all-to-all-done = bf16[128,2,16384]{2,1,0:T(2,128)(2,1)} async-done(((bf16[128,2,16384]{2,1,0:T(2,128)(2,1)}), bf16[128,2,16384]{2,1,0:T(2,128)(2,1)}, u32[]{:S(2)}, u32[]{:S(2)}) %all-to-all-start) | async-done | bytes 8388640 | tf_op jit(solution)/shard_map/all_to_all | solution.py:175
  551.4 13.1 %reshape.605 = bf16[256,16384]{1,0:T(8,128)(2,1)} reshape(bf16[128,2,16384]{2,1,0:T(2,128)(2,1)} %all-to-all-done) | data formatting | bytes 16777216 | tf_op jit(solution)/shard_map/reshape | solution.py:177
  564.5 7.4 gather_fusion
  573.3 1.5 fusion.11
  574.8 1.3 slice-done
  576.1 0.9 slice-done.1
  576.9 2.4 fusion.5
  579.3 2.1 fusion.14
  581.5 3.6 fusion.12
  585.1 2.9 multiply_reduce_fusion
  588.0 2.8 fusion.2
  590.8 1.1 fusion.62
  592.5 1.9 copy_dynamic-update-slice_fusion.1
  594.5 2.1 copy_dynamic-update-slice_fusion
  596.6 2.4 copy-done.4
  599.3 0.9 copy.365
  600.3 4.3 fusion.8
  604.6 1.4 copy-done.6
  606.8 2.9 bitcast_convert_fusion
  609.9 0.9 convert_element_type.141
  610.8 2.2 slice_bitcast_fusion.2
  613.0 1.7 fusion.53
  614.8 2.1 collective-permute-start.3
  616.9 3.7 collective-permute-start.2
  620.7 5.7 convolution_convert_fusion
  627.1 304.9 %all-gather.4.cloned.1.call-done = f32[256,2,64,4,128]{4,2,3,1,0:T(8,128)} async-done(((f32[2,2,64,4,128]{4,2,3,1,0:T(8,128)}), f32[256,2,64,4,128]{4,2,3,1,0:T(8,128)}) %all-gather.4.cloned.1.call-update) | async-done | bytes 67108880 | tf_op jit(solution)/shard_map/all_gather | solution.py:267
  932.0 21.7 %reduce_sum.79 = f32[2,2,64,4,128]{4,2,3,1,0:T(8,128)} reduce(f32[128,2,2,64,4,128]{5,3,4,2,1,0:T(8,128)} %bitcast.72, f32[]{:T(128)} %constant.174.clone.1), dimensions={0}, to_apply=%region_11.12 | reduce | flops 16646144 | bytes 67633152 | tf_op jit(solution)/shard_map/reduce_sum | solution.py:267
  953.7 14.1 %reshape.614 = bf16[128,2,16384]{2,1,0:T(2,128)(2,1)} reshape(bf16[256,16384]{1,0:T(8,128)(2,1)} %convolution_convert_fusion) | data formatting | bytes 16777216 | tf_op jit(solution)/shard_map/reshape | solution.py:272
  967.8 11.7 all-to-all-start.1
  979.6 3.2 copy.351
  982.7 2.6 reshape.608
  985.4 2.4 fusion.61
  988.8 2.1 fusion.55
  990.8 2.2 copy.388
  993.0 1.6 copy.387
  994.6 1.6 add_convert_fusion.1
  996.3 1.4 copy.373
  997.8 1.1 slice.227
  999.8 1.7 fusion.31
  1001.5 165.6 %all-to-all-done.1 = bf16[128,2,16384]{2,1,0:T(2,128)(2,1)} async-done(((bf16[128,2,16384]{2,1,0:T(2,128)(2,1)}), bf16[128,2,16384]{2,1,0:T(2,128)(2,1)}, u32[]{:S(2)}, u32[]{:S(2)}) %all-to-all-start.1) | async-done | bytes 8388640 | tf_op jit(solution)/shard_map/all_to_all | solution.py:271
  1167.1 13.1 %reshape.615 = bf16[256,16384]{1,0:T(8,128)(2,1)} reshape(bf16[128,2,16384]{2,1,0:T(2,128)(2,1)} %all-to-all-done.1) | data formatting | bytes 16777216 | tf_op jit(solution)/shard_map/reshape | solution.py:273
  1180.2 12.0 copy.366
  1192.2 5.9 fusion.17
  1200.9 0.8 copy.374
  (153 shorter events, 23.1 us)
Async XLA Ops:
  7.2 14.8 %copy-start.18 = (bf16[256,512]{1,0:T(8,128)(2,1)S(1)}, bf16[256,512]{1,0:T(8,128)(2,1)}, u32[]{:S(2)}) copy-start(bf16[256,512]{1,0:T(8,128)(2,1)} %param.13) | copy-start | bytes 786436
  7.2 10.9 copy-start.27
  7.2 384.2 %all-reduce.7.cloned.1.call-start = ((), (), s32[]{:S(2)}) async-start(), calls=%async_computation.3 | async-start | bytes 524288 | tf_op jit(solution)/shard_map/psum | solution.py:31
  10.5 16.2 %copy-start.22 = (s32[4,4,3]{1,0,2:T(4,128)S(1)}, s32[4,4,3]{1,0,2:T(4,128)}, u32[]{:S(2)}) copy-start(s32[4,4,3]{1,0,2:T(4,128)} %param.15) | copy-start | bytes 580
  11.5 377.4 %collective-permute-start = (bf16[2,64,512]{1,2,0:T(8,128)(2,1)}, bf16[2,64,512]{1,2,0:T(8,128)(2,1)}, u32[]{:S(2)}, u32[]{:S(2)}) collective-permute-start(bf16[2,64,512]{1,2,0:T(8,128)(2,1)} %get-tuple-element.106), channel_id=1, source_target_pairs={{0,2},{2,4},{4,6},{6,8},{8,10},{10,12},{12,14},{14,16},{16,18},{18... | collective-permute-start | bytes 393224 | tf_op jit(solution)/shard_map/ppermute | solution.py:23
  15.4 373.6 %collective-permute-start.1 = (bf16[2,64,512]{1,2,0:T(8,128)(2,1)}, bf16[2,64,512]{1,2,0:T(8,128)(2,1)}, u32[]{:S(2)}, u32[]{:S(2)}) collective-permute-start(bf16[2,64,512]{1,2,0:T(8,128)(2,1)} %get-tuple-element.107), channel_id=1, source_target_pairs={{2,0},{4,2},{6,4},{8,6},{10,8},{12,10},{14,12},{16,14},{18,16},{20... | collective-permute-start | bytes 393224 | tf_op jit(solution)/shard_map/ppermute | solution.py:24
  377.0 0.6 copy-start.19
  383.3 5.7 copy-start.20
  406.5 14.6 %copy-start.14 = (bf16[256,2048]{1,0:T(8,128)(2,1)S(1)}, bf16[256,2048]{1,0:T(8,128)(2,1)}, u32[]{:S(2)}) copy-start(bf16[256,2048]{1,0:T(8,128)(2,1)} %param.17) | copy-start | bytes 3145732
  406.5 16.1 %copy-start.15 = (bf16[256,2048]{1,0:T(8,128)(2,1)S(1)}, bf16[256,2048]{1,0:T(8,128)(2,1)}, u32[]{:S(2)}) copy-start(bf16[256,2048]{1,0:T(8,128)(2,1)} %param.11) | copy-start | bytes 3145732
  406.5 144.9 %all-to-all-start = ((bf16[128,2,16384]{2,1,0:T(2,128)(2,1)}), bf16[128,2,16384]{2,1,0:T(2,128)(2,1)}, u32[]{:S(2)}, u32[]{:S(2)}) async-start(bf16[128,2,16384]{2,1,0:T(2,128)(2,1)} %reshape.604), calls=%async_computation | async-start | bytes 16777216 | tf_op jit(solution)/shard_map/all_to_all | solution.py:175
  420.5 511.5 %all-gather.4.cloned.1.call-start = ((), (), s32[]{:S(2)}) async-start(), calls=%async_computation.2 | async-start | bytes 67633152 | tf_op jit(solution)/shard_map/all_gather | solution.py:267
  427.1 0.5 copy-start.25
  433.1 1.1 copy-start.5
  572.3 3.8 slice-start
  572.4 2.4 copy-start.8
  572.4 4.5 slice-start.1
  573.3 11.8 copy-start
  576.9 2.4 copy-start.12
  579.3 2.2 copy-start.16
  590.8 1.7 copy-start.2
  596.6 2.4 copy-start.4
  599.0 1.3 copy-start.26
  599.0 1.3 copy-start.17
  600.3 6.5 copy-start.1
  604.6 1.4 copy-start.6
  614.8 11.6 collective-permute-start.3
  616.9 9.5 collective-permute-start.2
  967.8 199.3 %all-to-all-start.1 = ((bf16[128,2,16384]{2,1,0:T(2,128)(2,1)}), bf16[128,2,16384]{2,1,0:T(2,128)(2,1)}, u32[]{:S(2)}, u32[]{:S(2)}) async-start(bf16[128,2,16384]{2,1,0:T(2,128)(2,1)} %reshape.614), calls=%async_computation.1 | async-start | bytes 16777216 | tf_op jit(solution)/shard_map/all_to_all | solution.py:271
  979.6 5.8 copy-start.3
  985.4 2.4 copy-start.7
  985.4 2.4 copy-start.9
  994.6 3.2 copy-start.10
  996.2 2.6 copy-start.11
  996.2 2.6 copy-start.23
  997.7 1.2 copy-start.13
  1180.2 12.0 copy-start.21
  1192.2 6.1 copy-start.24
Sparse Core Ops, SparseCore 0:
  26.7 218.4 all-reduce.6
  600.3 331.6 all-gather.3
